TPU v7x, 512 devices: a whole 4x4x16 slice. The times are simulated.
512 devices in a mesh: space: 32 (over z_lo, x), scal: 16 (over y, z_hi, core).
Axes of the slice: x: 4, y: 4, z: 16 (z_hi: 2, z_lo: 8; z = z_hi * 8 + z_lo), core: 2. Of those that a mesh axis runs over, the one named last changes fastest.
Arguments:
- scalars: float32 [512, 2048, 256], P('scal', 'space'), may hold values from -6 to 6
- schmidt: float32 [512], P('scal'), may hold values from 1 to 1000
- velocity_history: bfloat16 [32, 2, 256, 256], P('scal', None, 'space'), may hold values from -0.796875 to 0.796875
- fine_src: int32 [2048], replicated, may hold values from 0 to 254, as said below
- remap_weight: float32 [2048], replicated, may hold values from 0 to 1
- snap_step: int32 [2], replicated, may hold values from 0 to 31
Outputs:
- transported: float32 [512, 2048, 256], P('scal', 'space')
Inputs may be any that keep to these rules, and one draw needn't show every extreme that they name: fine_src may name any coarse row of any tile, in no particular order.
All inputs are finite; a program needn't handle non-finite values.
Results may differ from a plain program's by a relative error of at most 0.0003.
Values may be sent and summed in bfloat16 or wider, within the bound.
No kernel may reach another device: no remote copies, remote signals or barrier semaphores. Data moves between devices by JAX's collectives and lax.ppermute only.
A program may use at most 64 MiB of HBM per device.

v0:
```python
import jax
import jax.numpy as jnp
from jax import lax
from jax.sharding import PartitionSpec as P

STEPS = 2
diffusion_scale = 0.24


def from_root(value, axis, source):
    kept = jnp.where(lax.axis_index(axis) == source, value, 0).astype(value.dtype)
    return lax.psum(kept, axis)


def padded_2(cells, sides, width):
    for axis, dim in sides:
        count = lax.axis_size(axis)
        ends = count - 1
        head = lax.slice_in_dim(cells, 0, width, axis=dim)
        tail = lax.slice_in_dim(cells, cells.shape[dim] - width, cells.shape[dim], axis=dim)
        cells = jnp.concatenate(
            [
                lax.ppermute(tail, axis, [(i, (i + 1) % count) for i in range(ends)]),
                cells,
                lax.ppermute(head, axis, [((i + 1) % count, i) for i in range(ends)]),
            ],
            axis=dim,
        )
    return cells


def advance(padded, velocity, diffusivity):
    center = padded[:, 1:-1]
    upper_row = padded[:, 2:]
    lower_row = padded[:, :-2]
    east_cell = jnp.roll(center, -1, axis=2)
    west_cell = jnp.roll(center, 1, axis=2)
    laplacian = upper_row + lower_row + east_cell + west_cell - 4.0 * center
    return (
        center
        - velocity[0] * (0.5 * (upper_row - lower_row))
        - velocity[1] * (0.5 * (east_cell - west_cell))
        + diffusivity[:, None, None] * laplacian
    )


def body(scalars, schmidt, velocity_history, fine_src, remap_weight, snap_step):
    tile_rows = scalars.shape[1]
    snap_dev = velocity_history.shape[0]
    coarse_dev = velocity_history.shape[2]
    tile_count = lax.axis_size("space")
    coarse_total = coarse_dev * tile_count
    anchor = lax.axis_index("space") * tile_rows
    diffusivity = diffusion_scale / schmidt
    padded_src = jnp.pad(fine_src, (1, 1))
    padded_weight = jnp.pad(remap_weight, (1, 1))
    field = scalars
    for step_index in range(STEPS):
        padded = padded_2(field, (("space", 1),), 1)
        row_count = tile_rows + 2 * 0
        source_rows = lax.dynamic_slice_in_dim(padded_src, anchor + 1 - 0, row_count)
        weights = lax.dynamic_slice_in_dim(padded_weight, anchor + 1 - 0, row_count)
        coarse_index = lax.broadcasted_iota(jnp.int32, (row_count, coarse_total), 1)
        selection = jnp.where(
            coarse_index == source_rows[:, None], (1.0 - weights)[:, None], 0.0
        ) + jnp.where(coarse_index == source_rows[:, None] + 1, weights[:, None], 0.0)
        snapshot = snap_step[step_index]
        owner_index = snapshot // snap_dev
        own_slot = lax.dynamic_index_in_dim(
            velocity_history, snapshot % snap_dev, 0, keepdims=False
        )
        fine_velocity = jnp.einsum(
            "rn,cnz->crz",
            selection,
            lax.all_gather(own_slot, "space", axis=1, tiled=True).astype(jnp.float32),
            precision=lax.Precision.HIGHEST,
        )
        result_velocity = from_root(fine_velocity, "scal", owner_index)
        field = advance(padded, result_velocity, diffusivity)
    return field


def solution(mesh):
    return jax.shard_map(
        body,
        mesh=mesh,
        in_specs=(
            P("scal", "space", None),
            P("scal"),
            P("scal", None, "space", None),
            P(),
            P(),
            P(),
        ),
        out_specs=P("scal", "space", None),
        check_vma=False,
    )
```

profile of v0, /device:TPU:102, one launch (start us, length us, event | category | flops | bytes accessed | tf_op | source)
XLA Modules:
  0.0 541.2 jit_solution(13713053260277822044)
XLA Ops:
  6.5 1.1 fusion.25
  7.6 5.0 collective-permute-start.1
  12.6 1.9 collective-permute-start
  14.5 1.3 fusion.28
  21.0 0.8 broadcast_add_fusion
  21.7 0.8 broadcast_subtract_fusion
  22.5 0.8 constant_dynamic-slice_fusion
  23.3 71.4 %all-gather.1 = bf16[1,2,256,256]{3,2,1,0:T(8,128)(2,1)S(1)} all-gather(bf16[1,2,8,256]{3,2,1,0:T(8,128)(2,1)S(1)} %get-tuple-element.27), channel_id=3, replica_groups=mesh['space'=32,'scal'=16] {'space'}, dimensions={2}, use_global_device_ids=true | all-gather | bytes 270336 | tf_op jit(solution)/shard_map/all_gather | solution.py:75
  94.7 105.4 %all-gather = bf16[1,2,256,256]{3,2,1,0:T(8,128)(2,1)S(1)} all-gather(bf16[1,2,8,256]{3,2,1,0:T(8,128)(2,1)S(1)} %get-tuple-element.28), channel_id=2, replica_groups=mesh['space'=32,'scal'=16] {'space'}, dimensions={2}, use_global_device_ids=true | all-gather | bytes 270336 | tf_op jit(solution)/shard_map/all_gather | solution.py:75
  200.1 0.9 fusion
  201.1 0.9 fusion.1
  202.0 0.0 all-reduce.5.cloned.1.call-update
  202.0 0.0 copy-start
  202.0 5.1 fusion.26
  207.1 1.4 fusion.27
  208.5 303.0 %all-reduce.5.cloned.1.call-done = (f32[2,64,256]{2,1,0:T(8,128)}, f32[2,64,256]{2,1,0:T(8,128)}) async-done(((f32[2,64,256]{2,1,0:T(8,128)}, f32[2,64,256]{2,1,0:T(8,128)}), (f32[2,64,256]{2,1,0:T(8,128)}, f32[2,64,256]{2,1,0:T(8,128)})) %all-reduce.5.cloned.1.call-update) | async-done | bytes 262160 | tf_op jit(solution)/shard_map/psum | solution.py:12
  511.4 0.9 fusion.7
  512.4 3.8 multiply_add_fusion.1
  516.2 0.4 fusion.24
  516.6 0.7 fusion.23
  517.4 4.7 collective-permute-start.3
  522.1 1.9 collective-permute-start.2
  524.1 7.2 %collective-permute-done.2 = f32[32,1,256]{2,1,0:T(1,128)S(1)} collective-permute-done((f32[32,1,256]{2,1,0:T(1,128)S(1)}, f32[32,1,256]{2,1,0:T(1,128)S(1)}, u32[]{:S(2)}, u32[]{:S(2)}) %collective-permute-start.2) | collective-permute-done | bytes 32800 | tf_op jit(solution)/shard_map/ppermute | solution.py:25
  531.2 3.1 multiply_add_fusion
  (12 shorter events, 0.1 us)
Async XLA Ops:
  6.5 504.9 %all-reduce.5.cloned.1.call-start = ((), (), s32[]{:S(2)}) async-start(), calls=%async_computation | async-start | bytes 524288 | tf_op jit(solution)/shard_map/psum | solution.py:12
  7.6 504.7 %collective-permute-start.1 = (f32[32,1,256]{2,1,0:T(1,128)S(1)}, f32[32,1,256]{2,1,0:T(1,128)S(1)}, u32[]{:S(2)}, u32[]{:S(2)}) collective-permute-start(f32[32,1,256]{2,1,0:T(1,128)S(1)} %get-tuple-element.17), channel_id=1, source_target_pairs={{0,16},{16,32},{32,48},{48,64},{64,80},{80,96},{96,112},{112,128},... | collective-permute-start | bytes 98312 | tf_op jit(solution)/shard_map/ppermute | solution.py:23
  12.6 499.8 %collective-permute-start = (f32[32,1,256]{2,1,0:T(1,128)S(1)}, f32[32,1,256]{2,1,0:T(1,128)S(1)}, u32[]{:S(2)}, u32[]{:S(2)}) collective-permute-start(f32[32,1,256]{2,1,0:T(1,128)S(1)} %get-tuple-element.18), channel_id=1, source_target_pairs={{16,0},{32,16},{48,32},{64,48},{80,64},{96,80},{112,96},{128,112},... | collective-permute-start | bytes 98312 | tf_op jit(solution)/shard_map/ppermute | solution.py:25
  202.0 5.1 copy-start
  207.1 1.4 copy-start.2
  516.6 7.4 %copy-start.1 = (f32[2,64,256]{2,1,0:T(8,128)S(1)}, f32[2,64,256]{2,1,0:T(8,128)}, u32[]{:S(2)}) copy-start(f32[2,64,256]{2,1,0:T(8,128)} %get-tuple-element.6) | copy-start | bytes 393220
  517.4 6.7 %collective-permute-start.3 = (f32[32,1,256]{2,1,0:T(1,128)S(1)}, f32[32,1,256]{2,1,0:T(1,128)S(1)}, u32[]{:S(2)}, u32[]{:S(2)}) collective-permute-start(f32[32,1,256]{2,1,0:T(1,128)S(1)} %get-tuple-element.11), channel_id=1, source_target_pairs={{0,16},{16,32},{32,48},{48,64},{64,80},{80,96},{96,112},{112,128},... | collective-permute-start | bytes 98312 | tf_op jit(solution)/shard_map/ppermute | solution.py:23
  522.1 9.1 %collective-permute-start.2 = (f32[32,1,256]{2,1,0:T(1,128)S(1)}, f32[32,1,256]{2,1,0:T(1,128)S(1)}, u32[]{:S(2)}, u32[]{:S(2)}) collective-permute-start(f32[32,1,256]{2,1,0:T(1,128)S(1)} %get-tuple-element.12), channel_id=1, source_target_pairs={{16,0},{32,16},{48,32},{64,48},{80,64},{96,80},{112,96},{128,112},... | collective-permute-start | bytes 98312 | tf_op jit(solution)/shard_map/ppermute | solution.py:25
Sparse Core Ops, SparseCore 0:
  202.1 309.2 all-reduce.4
where the time goes:
time: 542 us; the launch traced here: 541 us
  waiting for transfers between devices  310 us (57%)
  blocking collectives  177 us (33%)
  between operations  18.7 us (3%)
  starting transfers between devices  13.5 us (2%)
  local copies, waits for them, and re-layouts  10.8 us (2%)
  other arithmetic  9.42 us (2%)
    psum x1, waiting for transfers between devices, from_root(): return lax.psum(kept, axis)  303 us
    all_gather x2, blocking collectives, body(): lax.all_gather(own_slot, 'space', axis=1, tiled=True).astype(jnp.float32)  177 us
  transfers between devices with their start and end apart: 5, of which 2 were waited for; matrix products, arithmetic and copies ran while one was open for 2% of the time, Pallas kernels for 0%

commit v1 on v0

--- a/solution.py
+++ b/solution.py
@@ -72,7 +72,10 @@
         fine_velocity = jnp.einsum(
             "rn,cnz->crz",
             selection,
-            lax.all_gather(own_slot, "space", axis=1, tiled=True).astype(jnp.float32),
+            jnp.concatenate(
+                lax.all_to_all(jnp.stack([own_slot] * lax.axis_size("space")), "space", 0, 0),
+                axis=1,
+            ).astype(jnp.float32),
             precision=lax.Precision.HIGHEST,
         )
         result_velocity = from_root(fine_velocity, "scal", owner_index)

time: 542 us -> 352 us (0.65)
  blocking collectives: 177 us -> 29.1 us
  waiting for transfers between devices: 310 us -> 258 us
  starting transfers between devices: 13.5 us -> 22.8 us
    all_gather x2 -> x0, blocking collectives: 177 us -> none  [body(): lax.all_gather(own_slot, 'space', axis=1, tiled=True).astype(jnp.float32)]
    psum x1, waiting for transfers between devices: 303 us -> 251 us  [from_root(): return lax.psum(kept, axis)]
    all_to_all x0 -> x1, blocking collectives: none -> 29.1 us  [body(): lax.all_to_all(jnp.stack([own_slot] * lax.axis_size('space')), 'space', 0...]
    all_to_all x0 -> x1, starting transfers between devices: none -> 9.67 us  [body(): lax.all_to_all(jnp.stack([own_slot] * lax.axis_size('space')), 'space', 0...]
  transfers between devices with their start and end apart: 5 -> 6, of which waited for: 2 -> 2; matrix products, arithmetic and copies ran while one was open for 2% -> 3% of each run, Pallas kernels for 0% -> 0%
where the time goes in v1:
time: 352 us
  waiting for transfers between devices  258 us (73%)
  blocking collectives  29.1 us (8%)
  starting transfers between devices  22.8 us (6%)
  between operations  18.7 us (5%)
  local copies, waits for them, and re-layouts  11.5 us (3%)
  other arithmetic  9.42 us (3%)
    psum x1, waiting for transfers between devices, from_root(): return lax.psum(kept, axis)  251 us
    all_to_all x1, blocking collectives, body(): lax.all_to_all(jnp.stack([own_slot] * lax.axis_size('space')), 'space', 0...  29.1 us
    all_to_all x1, starting transfers between devices, body(): lax.all_to_all(jnp.stack([own_slot] * lax.axis_size('space')), 'space', 0...  9.67 us
    ppermute x2, starting transfers between devices, padded_2(): lax.ppermute(tail, axis, [(i, (i + 1) % count) for i in range(ends)])  9.27 us
    slice x4, local copies, waits for them, and re-layouts, advance(): east_cell = jnp.roll(center, -1, axis=2)  7.57 us
    ppermute x2, waiting for transfers between devices, padded_2(): lax.ppermute(head, axis, [((i + 1) % count, i) for i in range(ends)])  7.16 us
  transfers between devices with their start and end apart: 6, of which 2 were waited for; matrix products, arithmetic and copies ran while one was open for 3% of the time, Pallas kernels for 0%

profile of v1, /device:TPU:102, one launch (start us, length us, event | category | flops | bytes accessed | tf_op | source)
XLA Modules:
  0.0 351.5 jit_solution(14106403213061034993)
XLA Ops:
  6.5 1.3 fusion.30
  11.7 0.8 dynamic-slice_bitcast_fusion
  12.5 29.1 %all_to_all.10 = bf16[32,2,8,256]{3,2,1,0:T(8,128)(2,1)S(1)} all-to-all(bf16[32,2,8,256]{3,2,1,0:T(8,128)(2,1)S(1)} %stack.5), channel_id=1, replica_groups=mesh['space'=32,'scal'=16] {'space'}, dimensions={0} | all-to-all | bytes 524288 | tf_op jit(solution)/shard_map/all_to_all | solution.py:76
  41.6 0.7 stack.4
  42.3 9.7 %all-to-all-start = ((bf16[32,2,8,256]{3,2,1,0:T(8,128)(2,1)}), bf16[32,2,8,256]{3,2,1,0:T(8,128)(2,1)S(1)}, u32[]{:S(2)}, u32[]{:S(2)}) async-start(bf16[32,2,8,256]{3,2,1,0:T(8,128)(2,1)} %stack.4), calls=%async_computation | async-start | bytes 524288 | tf_op jit(solution)/shard_map/all_to_all | solution.py:76
  52.0 0.0 all-reduce.5.cloned.1.call-start
  52.1 1.1 fusion.27
  53.2 4.6 %collective-permute-start.1 = (f32[32,1,256]{2,1,0:T(1,128)S(1)}, f32[32,1,256]{2,1,0:T(1,128)S(1)}, u32[]{:S(2)}, u32[]{:S(2)}) collective-permute-start(f32[32,1,256]{2,1,0:T(1,128)S(1)} %get-tuple-element.17), channel_id=1, source_target_pairs={{0,16},{16,32},{32,48},{48,64},{64,80},{80,96},{96,112},{112,128},... | collective-permute-start | bytes 98312 | tf_op jit(solution)/shard_map/ppermute | solution.py:23
  57.7 1.9 collective-permute-start
  61.0 0.8 broadcast_add_fusion
  61.8 0.8 broadcast_subtract_fusion
  62.6 5.1 %fusion.28 = (f32[32,64,255]{2,1,0:T(8,128)}, f32[32,64,255]{2,1,0:T(8,128)}) fusion(f32[32,64,256]{2,1,0:T(8,128)} %param.6), kind=kLoop, calls=%fused_computation.54 | loop fusion | bytes 8355840 | tf_op jit(solution)/shard_map/jit(_roll_static)/slice | solution.py:36
  67.6 0.9 fusion
  68.6 0.9 fusion.1
  69.5 1.4 fusion.29
  70.9 250.9 %all-reduce.5.cloned.1.call-done = (f32[2,64,256]{2,1,0:T(8,128)}, f32[2,64,256]{2,1,0:T(8,128)}) async-done(((f32[2,64,256]{2,1,0:T(8,128)}, f32[2,64,256]{2,1,0:T(8,128)}), (f32[2,64,256]{2,1,0:T(8,128)}, f32[2,64,256]{2,1,0:T(8,128)})) %all-reduce.5.cloned.1.call-update) | async-done | bytes 262160 | tf_op jit(solution)/shard_map/psum | solution.py:12
  321.8 0.9 fusion.9
  322.7 3.8 %multiply_add_fusion.1 = f32[32,64,256]{2,1,0:T(8,128)S(1)} fusion(f32[32,64,256]{2,1,0:T(8,128)S(1)} %copy-done, f32[32,64,255]{2,1,0:T(8,128)} %get-tuple-element.20, f32[32,64,1]{2,1,0:T(8,128)} %get-tuple-element.22, f32[32,64,1]{2,1,0:T(8,128)S(1)} %get-tuple-element.21, f32[32,64,255]{2,1,0:T(8,128)} %get-tuple-element.19, ...), kind=kLoop, calls=%fused_computation.9 | loop fusion | flops 8912896 | bytes 8585344 | tf_op jit(solution)/shard_map/add | solution.py:40
  326.6 0.4 fusion.26
  327.0 0.7 fusion.25
  327.7 4.7 %collective-permute-start.3 = (f32[32,1,256]{2,1,0:T(1,128)S(1)}, f32[32,1,256]{2,1,0:T(1,128)S(1)}, u32[]{:S(2)}, u32[]{:S(2)}) collective-permute-start(f32[32,1,256]{2,1,0:T(1,128)S(1)} %get-tuple-element.11), channel_id=1, source_target_pairs={{0,16},{16,32},{32,48},{48,64},{64,80},{80,96},{96,112},{112,128},... | collective-permute-start | bytes 98312 | tf_op jit(solution)/shard_map/ppermute | solution.py:23
  332.4 1.9 collective-permute-start.2
  334.4 7.2 %collective-permute-done.2 = f32[32,1,256]{2,1,0:T(1,128)S(1)} collective-permute-done((f32[32,1,256]{2,1,0:T(1,128)S(1)}, f32[32,1,256]{2,1,0:T(1,128)S(1)}, u32[]{:S(2)}, u32[]{:S(2)}) %collective-permute-start.2) | collective-permute-done | bytes 32800 | tf_op jit(solution)/shard_map/ppermute | solution.py:25
  341.5 3.1 multiply_add_fusion
  (15 shorter events, 0.1 us)
Async XLA Ops:
  42.3 26.2 %all-to-all-start = ((bf16[32,2,8,256]{3,2,1,0:T(8,128)(2,1)}), bf16[32,2,8,256]{3,2,1,0:T(8,128)(2,1)S(1)}, u32[]{:S(2)}, u32[]{:S(2)}) async-start(bf16[32,2,8,256]{3,2,1,0:T(8,128)(2,1)} %stack.4), calls=%async_computation | async-start | bytes 524288 | tf_op jit(solution)/shard_map/all_to_all | solution.py:76
  52.0 269.7 %all-reduce.5.cloned.1.call-start = ((), (), s32[]{:S(2)}) async-start(), calls=%async_computation.2 | async-start | bytes 524288 | tf_op jit(solution)/shard_map/psum | solution.py:12
  53.2 269.5 %collective-permute-start.1 = (f32[32,1,256]{2,1,0:T(1,128)S(1)}, f32[32,1,256]{2,1,0:T(1,128)S(1)}, u32[]{:S(2)}, u32[]{:S(2)}) collective-permute-start(f32[32,1,256]{2,1,0:T(1,128)S(1)} %get-tuple-element.17), channel_id=1, source_target_pairs={{0,16},{16,32},{32,48},{48,64},{64,80},{80,96},{96,112},{112,128},... | collective-permute-start | bytes 98312 | tf_op jit(solution)/shard_map/ppermute | solution.py:23
  57.7 264.9 %collective-permute-start = (f32[32,1,256]{2,1,0:T(1,128)S(1)}, f32[32,1,256]{2,1,0:T(1,128)S(1)}, u32[]{:S(2)}, u32[]{:S(2)}) collective-permute-start(f32[32,1,256]{2,1,0:T(1,128)S(1)} %get-tuple-element.18), channel_id=1, source_target_pairs={{16,0},{32,16},{48,32},{64,48},{80,64},{96,80},{112,96},{128,112},... | collective-permute-start | bytes 98312 | tf_op jit(solution)/shard_map/ppermute | solution.py:25
  62.6 7.0 %copy-start = (f32[32,64,256]{2,1,0:T(8,128)S(1)}, f32[32,64,256]{2,1,0:T(8,128)}, u32[]{:S(2)}) copy-start(f32[32,64,256]{2,1,0:T(8,128)} %param.6) | copy-start | bytes 6291460
  69.5 1.4 copy-start.2
  327.0 7.4 %copy-start.1 = (f32[2,64,256]{2,1,0:T(8,128)S(1)}, f32[2,64,256]{2,1,0:T(8,128)}, u32[]{:S(2)}) copy-start(f32[2,64,256]{2,1,0:T(8,128)} %get-tuple-element.6) | copy-start | bytes 393220
  327.7 6.7 %collective-permute-start.3 = (f32[32,1,256]{2,1,0:T(1,128)S(1)}, f32[32,1,256]{2,1,0:T(1,128)S(1)}, u32[]{:S(2)}, u32[]{:S(2)}) collective-permute-start(f32[32,1,256]{2,1,0:T(1,128)S(1)} %get-tuple-element.11), channel_id=1, source_target_pairs={{0,16},{16,32},{32,48},{48,64},{64,80},{80,96},{96,112},{112,128},... | collective-permute-start | bytes 98312 | tf_op jit(solution)/shard_map/ppermute | solution.py:23
  332.4 9.1 %collective-permute-start.2 = (f32[32,1,256]{2,1,0:T(1,128)S(1)}, f32[32,1,256]{2,1,0:T(1,128)S(1)}, u32[]{:S(2)}, u32[]{:S(2)}) collective-permute-start(f32[32,1,256]{2,1,0:T(1,128)S(1)} %get-tuple-element.12), channel_id=1, source_target_pairs={{16,0},{32,16},{48,32},{64,48},{80,64},{96,80},{112,96},{128,112},... | collective-permute-start | bytes 98312 | tf_op jit(solution)/shard_map/ppermute | solution.py:25
Sparse Core Ops, SparseCore 0:
  69.6 252.0 all-reduce.4

commit v2 on v0

--- a/solution.py
+++ b/solution.py
@@ -9,7 +9,7 @@
 
 def from_root(value, axis, source):
     kept = jnp.where(lax.axis_index(axis) == source, value, 0).astype(value.dtype)
-    return lax.psum(kept, axis)
+    return jnp.sum(lax.all_gather(kept, axis), axis=0)
 
 
 def padded_2(cells, sides, width):

time: 542 us -> 381 us (0.70)
  the two profiles are of different devices: /device:TPU:102 before, /device:TPU:6 now
where the time goes in v2:
time: 381 us
  blocking collectives  236 us (62%)
  waiting for transfers between devices  79.4 us (21%)
  between operations  18.3 us (5%)
  other arithmetic  16.3 us (4%)
  starting transfers between devices  15.5 us (4%)
  local copies, waits for them, and re-layouts  13.3 us (3%)
    all_gather x2, blocking collectives, body(): lax.all_gather(own_slot, 'space', axis=1, tiled=True).astype(jnp.float32)  236 us
    all_gather x2, waiting for transfers between devices, from_root(): return jnp.sum(lax.all_gather(kept, axis), axis=0)  75.4 us
    ppermute x2, starting transfers between devices, padded_2(): lax.ppermute(head, axis, [((i + 1) % count, i) for i in range(ends)])  11.6 us
    add x2, other arithmetic, advance(): center - velocity[0] * (0.5 * (upper_row - lower_row))  10.6 us
    slice x4, local copies, waits for them, and re-layouts, advance(): east_cell = jnp.roll(center, -1, axis=2)  10.1 us
  transfers between devices with their start and end apart: 6, of which 2 were waited for; matrix products, arithmetic and copies ran while one was open for 5% of the time, Pallas kernels for 0%

profile of v2, /device:TPU:6, one launch (start us, length us, event | category | flops | bytes accessed | tf_op | source)
XLA Modules:
  0.0 380.8 jit_solution(4475491553548812360)
XLA Ops:
  6.5 1.3 fusion.28
  12.0 0.8 broadcast_add_fusion
  12.8 0.8 broadcast_subtract_fusion
  13.6 0.8 constant_dynamic-slice_fusion
  14.3 109.1 %all-gather = bf16[1,2,256,256]{3,2,1,0:T(8,128)(2,1)S(1)} all-gather(bf16[1,2,8,256]{3,2,1,0:T(8,128)(2,1)S(1)} %get-tuple-element.26), channel_id=2, replica_groups=mesh['space'=32,'scal'=16] {'space'}, dimensions={2}, use_global_device_ids=true | all-gather | bytes 270336 | tf_op jit(solution)/shard_map/all_gather | solution.py:75
  123.4 0.9 fusion.1
  125.1 126.9 %all-gather.2 = bf16[1,2,256,256]{3,2,1,0:T(8,128)(2,1)S(1)} all-gather(bf16[1,2,8,256]{3,2,1,0:T(8,128)(2,1)S(1)} %get-tuple-element.25), channel_id=4, replica_groups=mesh['space'=32,'scal'=16] {'space'}, dimensions={2}, use_global_device_ids=true | all-gather | bytes 270336 | tf_op jit(solution)/shard_map/all_gather | solution.py:75
  252.0 0.9 fusion
  253.0 1.1 fusion.25
  254.1 1.9 collective-permute-start.1
  256.0 7.7 %collective-permute-start = (f32[32,1,256]{2,1,0:T(1,128)S(1)}, f32[32,1,256]{2,1,0:T(1,128)S(1)}, u32[]{:S(2)}, u32[]{:S(2)}) collective-permute-start(f32[32,1,256]{2,1,0:T(1,128)S(1)} %get-tuple-element.16), channel_id=1, source_target_pairs={{16,0},{32,16},{48,32},{64,48},{80,64},{96,80},{112,96},{128,112},... | collective-permute-start | bytes 98312 | tf_op jit(solution)/shard_map/ppermute | solution.py:25
  263.8 0.7 broadcast_divide_fusion
  264.4 3.1 fusion.27
  267.5 2.8 fusion.26
  270.3 1.7 reduce_sum.18
  272.1 5.9 %multiply_add_fusion.1 = f32[32,64,256]{2,1,0:T(8,128)S(1)} fusion(f32[32,64,256]{2,1,0:T(8,128)} %param.6, f32[32,64,255]{2,1,0:T(8,128)} %get-tuple-element.18, f32[32,64,1]{2,1,0:T(8,128)} %get-tuple-element.20, f32[32,64,1]{2,1,0:T(8,128)S(1)} %get-tuple-element.19, f32[32,64,255]{2,1,0:T(8,128)} %get-tuple-element.17, ...), kind=kLoop, calls=%fused_computation.9 | loop fusion | flops 8912896 | bytes 8585344 | tf_op jit(solution)/shard_map/add | solution.py:40
  278.0 1.4 fusion.24
  279.4 2.8 fusion.23
  282.2 75.4 %all-gather.9.cloned.1.call-done = f32[32,64,256]{2,1,0:T(8,128)} async-done(((f32[2,64,256]{2,1,0:T(8,128)}), f32[32,64,256]{2,1,0:T(8,128)}) %all-gather.9.cloned.1.call-update) | async-done | bytes 2097168 | tf_op jit(solution)/shard_map/all_gather | solution.py:12
  357.7 1.7 reduce_sum.19
  359.4 1.9 collective-permute-start.3
  361.3 3.9 %collective-permute-start.2 = (f32[32,1,256]{2,1,0:T(1,128)S(1)}, f32[32,1,256]{2,1,0:T(1,128)S(1)}, u32[]{:S(2)}, u32[]{:S(2)}) collective-permute-start(f32[32,1,256]{2,1,0:T(1,128)S(1)} %get-tuple-element.10), channel_id=1, source_target_pairs={{16,0},{32,16},{48,32},{64,48},{80,64},{96,80},{112,96},{128,112},... | collective-permute-start | bytes 98312 | tf_op jit(solution)/shard_map/ppermute | solution.py:25
  365.3 4.0 %collective-permute-done.2 = f32[32,1,256]{2,1,0:T(1,128)S(1)} collective-permute-done((f32[32,1,256]{2,1,0:T(1,128)S(1)}, f32[32,1,256]{2,1,0:T(1,128)S(1)}, u32[]{:S(2)}, u32[]{:S(2)}) %collective-permute-start.2) | collective-permute-done | bytes 32800 | tf_op jit(solution)/shard_map/ppermute | solution.py:25
  369.2 4.8 %multiply_add_fusion = f32[32,64,256]{2,1,0:T(8,128)} fusion(f32[32,64,256]{2,1,0:T(8,128)S(1)} %multiply_add_fusion.1, f32[32,64,255]{2,1,0:T(8,128)} %get-tuple-element.12, f32[32,64,1]{2,1,0:T(8,128)} %get-tuple-element.14, f32[32,64,1]{2,1,0:T(8,128)S(1)} %get-tuple-element.13, f32[32,64,255]{2,1,0:T(8,128)} %get-tuple-element.11, ...), kind=kLoop, calls=%fused_computation.8 | loop fusion | flops 8912896 | bytes 8585344 | tf_op jit(solution)/shard_map/add | solution.py:40
  (13 shorter events, 0.2 us)
Async XLA Ops:
  6.5 263.8 %all-gather.7.cloned.1.call-start = ((), (), s32[]{:S(2)}) async-start(), calls=%async_computation | async-start | bytes 2228224 | tf_op jit(solution)/shard_map/all_gather | solution.py:12
  124.4 233.3 %all-gather.9.cloned.1.call-start = ((), (), s32[]{:S(2)}) async-start(), calls=%async_computation.1 | async-start | bytes 2228224 | tf_op jit(solution)/shard_map/all_gather | solution.py:12
  254.1 18.0 %collective-permute-start.1 = (f32[32,1,256]{2,1,0:T(1,128)S(1)}, f32[32,1,256]{2,1,0:T(1,128)S(1)}, u32[]{:S(2)}, u32[]{:S(2)}) collective-permute-start(f32[32,1,256]{2,1,0:T(1,128)S(1)} %get-tuple-element.15), channel_id=1, source_target_pairs={{0,16},{16,32},{32,48},{48,64},{64,80},{80,96},{96,112},{112,128},... | collective-permute-start | bytes 98312 | tf_op jit(solution)/shard_map/ppermute | solution.py:23
  256.0 16.0 %collective-permute-start = (f32[32,1,256]{2,1,0:T(1,128)S(1)}, f32[32,1,256]{2,1,0:T(1,128)S(1)}, u32[]{:S(2)}, u32[]{:S(2)}) collective-permute-start(f32[32,1,256]{2,1,0:T(1,128)S(1)} %get-tuple-element.16), channel_id=1, source_target_pairs={{16,0},{32,16},{48,32},{64,48},{80,64},{96,80},{112,96},{128,112},... | collective-permute-start | bytes 98312 | tf_op jit(solution)/shard_map/ppermute | solution.py:25
  264.4 3.1 copy-start
  359.4 5.9 %collective-permute-start.3 = (f32[32,1,256]{2,1,0:T(1,128)S(1)}, f32[32,1,256]{2,1,0:T(1,128)S(1)}, u32[]{:S(2)}, u32[]{:S(2)}) collective-permute-start(f32[32,1,256]{2,1,0:T(1,128)S(1)} %get-tuple-element.9), channel_id=1, source_target_pairs={{0,16},{16,32},{32,48},{48,64},{64,80},{80,96},{96,112},{112,128},... | collective-permute-start | bytes 98312 | tf_op jit(solution)/shard_map/ppermute | solution.py:23
  361.3 7.9 %collective-permute-start.2 = (f32[32,1,256]{2,1,0:T(1,128)S(1)}, f32[32,1,256]{2,1,0:T(1,128)S(1)}, u32[]{:S(2)}, u32[]{:S(2)}) collective-permute-start(f32[32,1,256]{2,1,0:T(1,128)S(1)} %get-tuple-element.10), channel_id=1, source_target_pairs={{16,0},{32,16},{48,32},{64,48},{80,64},{96,80},{112,96},{128,112},... | collective-permute-start | bytes 98312 | tf_op jit(solution)/shard_map/ppermute | solution.py:25
Sparse Core Ops, SparseCore 0:
  124.5 104.0 all-gather.6
  253.1 104.4 all-gather.8
